TPU v7x, 32 devices: a whole 2x2x4 slice. The times are simulated.
32 devices in a mesh: dp: 4 (over x, core), seq: 8 (over z, y).
Axes of the slice: x: 2, y: 2, z: 4, core: 2. Of those that a mesh axis runs over, the one named last changes fastest.
Arguments:
- inputs: bfloat16 [2, 4, 1024, 768], P(None, 'dp', 'seq'), may hold values from -6 to 6
- cotangent: bfloat16 [2, 4, 1024, 768], P(None, 'dp', 'seq'), may hold values from -6 to 6
- bounds: int32 [2, 4, 2, 2], P(None, 'dp'), may hold values from 0 to 1024, as said below
- ln1_gain: bfloat16 [768], P(('dp', 'seq')), may hold values from 0.5 to 1.5
- ln1_bias: bfloat16 [768], P(('dp', 'seq')), may hold values from -1 to 1
- w_qkv: bfloat16 [768, 2304], P(('dp', 'seq')), may hold values from -0.21875 to 0.21875
- b_query: bfloat16 [768], P(('dp', 'seq')), may hold values from -1.5 to 1.5
- b_value: bfloat16 [768], P(('dp', 'seq')), may hold values from -1.5 to 1.5
- w_out: bfloat16 [768, 768], P(('dp', 'seq')), may hold values from -1.25 to 1.25
- b_out: bfloat16 [768], P(('dp', 'seq')), may hold values from -1.5 to 1.5
- ln2_gain: bfloat16 [768], P(('dp', 'seq')), may hold values from 0.5 to 1.5
- ln2_bias: bfloat16 [768], P(('dp', 'seq')), may hold values from -1 to 1
- w_up: bfloat16 [768, 3072], P(('dp', 'seq')), may hold values from -0.21875 to 0.21875
- b_up: bfloat16 [3072], P(('dp', 'seq')), may hold values from -1.5 to 1.5
- w_down: bfloat16 [3072, 768], P(('dp', 'seq')), may hold values from -0.109375 to 0.109375
- b_down: bfloat16 [768], P(('dp', 'seq')), may hold values from -1.5 to 1.5
Outputs:
- outputs: bfloat16 [2, 4, 1024, 768], P(None, 'dp', 'seq')
- input_grad: bfloat16 [2, 4, 1024, 768], P(None, 'dp', 'seq')
- grad_ln1_gain: float32 [768], P(('dp', 'seq'))
- grad_ln1_bias: float32 [768], P(('dp', 'seq'))
- grad_w_qkv: float32 [768, 2304], P(('dp', 'seq'))
- grad_b_query: float32 [768], P(('dp', 'seq'))
- grad_b_value: float32 [768], P(('dp', 'seq'))
- grad_w_out: float32 [768, 768], P(('dp', 'seq'))
- grad_b_out: float32 [768], P(('dp', 'seq'))
- grad_ln2_gain: float32 [768], P(('dp', 'seq'))
- grad_ln2_bias: float32 [768], P(('dp', 'seq'))
- grad_w_up: float32 [768, 3072], P(('dp', 'seq'))
- grad_b_up: float32 [3072], P(('dp', 'seq'))
- grad_w_down: float32 [3072, 768], P(('dp', 'seq'))
- grad_b_down: float32 [768], P(('dp', 'seq'))
Inputs may be any that keep to these rules, and one draw needn't show every extreme that they name: `bounds`: for each sequence, 2 picture pieces [start, end) of exactly 256 rows each, in increasing order and not intersecting.
All inputs are finite; a program needn't handle non-finite values.
Results may differ from a plain program's by a relative error of at most 0.02.
Values may be sent and summed in bfloat16 or wider, within the bound.
No kernel may reach another device: no remote copies, remote signals or barrier semaphores. Data moves between devices by JAX's collectives and lax.ppermute only.
A program may use at most 256 MiB of HBM per device.

v0:
```python
from functools import partial

import jax
import jax.numpy as jnp
from jax import lax
from jax.sharding import PartitionSpec as P

HEADS = 12
HEAD = 64


EPSILON = 1e-05


def layer_norm(values, ln_gain, ln_shift):
    center = jnp.mean(values, axis=-1, keepdims=True)
    centered = values - center
    spread = jnp.mean(centered * centered, axis=-1, keepdims=True)
    return centered * lax.rsqrt(spread + EPSILON) * ln_gain + ln_shift


def piece_label(positions, bounds):
    inside = (positions[:, None] >= bounds[None, :, 0]) & (positions[:, None] < bounds[None, :, 1])
    labels = jnp.arange(1, bounds.shape[0] + 1, dtype=jnp.int32)
    return jnp.sum(jnp.where(inside, labels[None, :], 0), axis=1) - 1


def allowed_mask(query_pos, key_pos, bounds):
    query_label = piece_label(query_pos, bounds)
    key_label = piece_label(key_pos, bounds)
    causal = key_pos[None, :] <= query_pos[:, None]
    same_piece = (query_label[:, None] == key_label[None, :]) & (query_label[:, None] >= 0)
    return causal | same_piece


def outer_rows(left, right):
    return lax.dot_general(
        left, right, (((0,), (0,)), ((), ())), preferred_element_type=jnp.float32
    )


def times_transposed(left, right):
    return lax.dot_general(
        left, right, (((1,), (1,)), ((), ())), preferred_element_type=jnp.float32
    )


def key_step():
    return 512


def masked_weights(query_heads, key_heads, query_pos, key_pos, bounds):
    factor = query_heads.shape[2] ** (-0.5)
    scores = (
        jnp.einsum("rhd,khd->hrk", query_heads, key_heads, preferred_element_type=jnp.float32)
        * factor
    )
    allowed = allowed_mask(query_pos, key_pos, bounds)
    return jnp.where(allowed[None], jnp.exp(scores), 0.0)


def forward_fold(query_heads, query_pos, bounds):
    head_count = query_heads.shape[1]

    def fold_keys(carry, piece, first_row):
        key_piece, value_piece = piece
        piece_len = key_piece.shape[0]
        step_len = key_step()

        def inner_step(block_idx, partial_sums):
            weighted, totals = partial_sums
            offset = block_idx * step_len
            key_heads = lax.dynamic_slice_in_dim(key_piece, offset, step_len, 0).reshape(
                step_len, head_count, -1
            )
            value_heads = lax.dynamic_slice_in_dim(value_piece, offset, step_len, 0).reshape(
                step_len, head_count, -1
            )
            key_pos = offset + jnp.arange(step_len, dtype=jnp.int32)
            weights = masked_weights(query_heads, key_heads, query_pos, key_pos, bounds)
            weighted = weighted + jnp.einsum(
                "hrk,khd->rhd",
                weights.astype(jnp.bfloat16),
                value_heads,
                preferred_element_type=jnp.float32,
            )
            return (weighted, totals + jnp.sum(weights, axis=-1))

        return lax.fori_loop(0, piece_len // step_len, inner_step, carry)

    return fold_keys


def backward_fold(query_heads, query_pos, bounds, grad_heads, delta):
    head_count = query_heads.shape[1]
    factor = query_heads.shape[2] ** (-0.5)

    def fold_grads(carry, piece, first_row):
        key_piece, value_piece = piece
        piece_len = key_piece.shape[0]
        step_len = key_step()

        def inner_step(block_idx, partial_sums):
            query_grad, key_grad, value_grad = partial_sums
            offset = block_idx * step_len
            key_heads = lax.dynamic_slice_in_dim(key_piece, offset, step_len, 0).reshape(
                step_len, head_count, -1
            )
            value_heads = lax.dynamic_slice_in_dim(value_piece, offset, step_len, 0).reshape(
                step_len, head_count, -1
            )
            key_pos = offset + jnp.arange(step_len, dtype=jnp.int32)
            weights = masked_weights(query_heads, key_heads, query_pos, key_pos, bounds)
            products = jnp.einsum(
                "rhd,khd->hrk", grad_heads, value_heads, preferred_element_type=jnp.float32
            )
            score_grad = (weights * (products - delta[:, :, None])).astype(jnp.bfloat16)
            query_grad = (
                query_grad
                + jnp.einsum(
                    "hrk,khd->rhd", score_grad, key_heads, preferred_element_type=jnp.float32
                )
                * factor
            )
            key_rows = (
                jnp.einsum(
                    "hrk,rhd->khd", score_grad, query_heads, preferred_element_type=jnp.float32
                )
                * factor
            ).reshape(step_len, -1)
            value_rows = jnp.einsum(
                "hrk,rhd->khd",
                weights.astype(jnp.bfloat16),
                grad_heads,
                preferred_element_type=jnp.float32,
            ).reshape(step_len, -1)
            key_grad = lax.dynamic_update_slice_in_dim(key_grad, key_rows, offset, 0)
            value_grad = lax.dynamic_update_slice_in_dim(value_grad, value_rows, offset, 0)
            return (query_grad, key_grad, value_grad)

        return lax.fori_loop(0, piece_len // step_len, inner_step, carry)

    return fold_grads


def body(
    inputs,
    cotangent,
    bounds,
    ln1_gain,
    ln1_bias,
    w_qkv,
    b_query,
    b_value,
    w_out,
    b_out,
    ln2_gain,
    ln2_bias,
    w_up,
    b_up,
    w_down,
    b_down,
):
    shards = (
        ln1_gain,
        ln1_bias,
        w_qkv,
        b_query,
        b_value,
        w_out,
        b_out,
        ln2_gain,
        ln2_bias,
        w_up,
        b_up,
        w_down,
        b_down,
    )
    micro_count = inputs.shape[0]
    row_count = inputs.shape[2]
    width = inputs.shape[3]
    total_len = row_count * lax.axis_size("seq")
    query_pos = lax.axis_index("seq") * row_count + jnp.arange(row_count, dtype=jnp.int32)
    grad_sums = [None] * 13
    outputs_list = []
    input_grads = []
    for micro_idx in range(micro_count):
        gathered = (
            lax.all_gather(shards[0], ("dp", "seq"), axis=0, tiled=True),
            lax.all_gather(shards[1], ("dp", "seq"), axis=0, tiled=True),
            lax.all_gather(shards[2], ("dp", "seq"), axis=0, tiled=True),
            lax.all_gather(shards[3], ("dp", "seq"), axis=0, tiled=True),
            lax.all_gather(shards[4], ("dp", "seq"), axis=0, tiled=True),
            lax.all_gather(shards[5], ("dp", "seq"), axis=0, tiled=True),
            lax.all_gather(shards[6], ("dp", "seq"), axis=0, tiled=True),
            lax.all_gather(shards[7], ("dp", "seq"), axis=0, tiled=True),
            lax.all_gather(shards[8], ("dp", "seq"), axis=0, tiled=True),
            lax.all_gather(shards[9], ("dp", "seq"), axis=0, tiled=True),
            lax.all_gather(shards[10], ("dp", "seq"), axis=0, tiled=True),
            lax.all_gather(shards[11], ("dp", "seq"), axis=0, tiled=True),
            lax.all_gather(shards[12], ("dp", "seq"), axis=0, tiled=True),
        )
        (
            gain_one,
            shift_one,
            proj_qkv,
            bias_query,
            bias_value,
            proj_out,
            bias_out,
            gain_two,
            shift_two,
            proj_up,
            bias_up,
            proj_down,
            bias_down,
        ) = gathered
        seq_bounds = bounds[micro_idx, 0]
        seq_in = inputs[micro_idx, 0].astype(jnp.float32)
        normed_f, norm_one_back = jax.vjp(
            layer_norm, seq_in, gain_one.astype(jnp.float32), shift_one.astype(jnp.float32)
        )
        normed = normed_f.astype(jnp.bfloat16)
        projected = jnp.dot(normed, proj_qkv, preferred_element_type=jnp.float32)
        queries = (projected[:, :width] + bias_query.astype(jnp.float32)).astype(jnp.bfloat16)
        keys_now = projected[:, width : 2 * width].astype(jnp.bfloat16)
        values_now = (projected[:, 2 * width :] + bias_value.astype(jnp.float32)).astype(
            jnp.bfloat16
        )
        query_heads = queries.reshape(row_count, HEADS, HEAD)
        start_sums = (
            jnp.zeros((row_count, HEADS, HEAD), jnp.float32),
            jnp.zeros((HEADS, row_count), jnp.float32),
        )
        fold_keys = forward_fold(query_heads, query_pos, seq_bounds)
        weighted, totals = fold_keys(
            start_sums,
            (
                lax.all_gather(keys_now, "seq", axis=0, tiled=True),
                lax.all_gather(values_now, "seq", axis=0, tiled=True),
            ),
            jnp.int32(0),
        )
        attended = weighted / totals.T[:, :, None]
        attended_b = attended.reshape(row_count, width).astype(jnp.bfloat16)
        branch = jnp.dot(
            attended_b, proj_out, preferred_element_type=jnp.float32
        ) + bias_out.astype(jnp.float32)
        middle = seq_in + branch
        normed_two_f, norm_two_back = jax.vjp(
            layer_norm, middle, gain_two.astype(jnp.float32), shift_two.astype(jnp.float32)
        )
        normed_two = normed_two_f.astype(jnp.bfloat16)
        hidden = jnp.dot(normed_two, proj_up, preferred_element_type=jnp.float32) + bias_up.astype(
            jnp.float32
        )
        activated_f, gelu_back = jax.vjp(partial(jax.nn.gelu, approximate=False), hidden)
        activated = activated_f.astype(jnp.bfloat16)
        mlp_out = jnp.dot(
            activated, proj_down, preferred_element_type=jnp.float32
        ) + bias_down.astype(jnp.float32)
        outputs_list.append((middle + mlp_out).astype(jnp.bfloat16))
        qkv_back, out_back, up_back, down_back = (
            lax.all_gather(w_qkv, ("dp", "seq"), axis=0, tiled=True),
            lax.all_gather(w_out, ("dp", "seq"), axis=0, tiled=True),
            lax.all_gather(w_up, ("dp", "seq"), axis=0, tiled=True),
            lax.all_gather(w_down, ("dp", "seq"), axis=0, tiled=True),
        )
        out_grad = cotangent[micro_idx, 0]
        out_grad_f = out_grad.astype(jnp.float32)
        grad_down = outer_rows(activated, out_grad)
        grad_bias_down = jnp.sum(out_grad_f, axis=0)
        act_grad = times_transposed(out_grad, down_back)
        (hidden_grad,) = gelu_back(act_grad)
        hidden_grad_b = hidden_grad.astype(jnp.bfloat16)
        grad_up = outer_rows(normed_two, hidden_grad_b)
        grad_bias_up = jnp.sum(hidden_grad_b.astype(jnp.float32), axis=0)
        normed_two_grad = times_transposed(hidden_grad_b, up_back)
        middle_ln_grad, grad_gain_two, grad_shift_two = norm_two_back(normed_two_grad)
        middle_grad = out_grad_f + middle_ln_grad
        branch_grad = middle_grad.astype(jnp.bfloat16)
        grad_out = outer_rows(attended_b, branch_grad)
        grad_bias_out = jnp.sum(branch_grad.astype(jnp.float32), axis=0)
        attended_grad = times_transposed(branch_grad, out_back).astype(jnp.bfloat16)
        attended_grad_f = attended_grad.astype(jnp.float32).reshape(row_count, HEADS, HEAD)
        delta = jnp.sum(attended_grad_f * attended, axis=-1).T / totals
        grad_heads = (attended_grad_f / totals.T[:, :, None]).astype(jnp.bfloat16)
        start_grads = (
            jnp.zeros((row_count, HEADS, HEAD), jnp.float32),
            jnp.zeros((total_len, width), jnp.float32),
            jnp.zeros((total_len, width), jnp.float32),
        )
        fold_grads = backward_fold(query_heads, query_pos, seq_bounds, grad_heads, delta)
        folded = fold_grads(
            start_grads,
            (
                lax.all_gather(keys_now, "seq", axis=0, tiled=True),
                lax.all_gather(values_now, "seq", axis=0, tiled=True),
            ),
            jnp.int32(0),
        )
        query_grad = folded[0]
        key_own, value_own = (
            lax.psum_scatter(
                folded[1].astype(jnp.bfloat16), "seq", scatter_dimension=0, tiled=True
            ).astype(jnp.float32),
            lax.psum_scatter(
                folded[2].astype(jnp.bfloat16), "seq", scatter_dimension=0, tiled=True
            ).astype(jnp.float32),
        )
        query_grad_b = query_grad.reshape(row_count, width).astype(jnp.bfloat16)
        key_grad_b = key_own.astype(jnp.bfloat16)
        value_grad_b = value_own.astype(jnp.bfloat16)
        proj_grad = jnp.concatenate([query_grad_b, key_grad_b, value_grad_b], axis=1)
        grad_qkv = outer_rows(normed, proj_grad)
        grad_bias_query = jnp.sum(query_grad_b.astype(jnp.float32), axis=0)
        grad_bias_value = jnp.sum(value_grad_b.astype(jnp.float32), axis=0)
        normed_grad = times_transposed(proj_grad, qkv_back)
        input_ln_grad, grad_gain_one, grad_shift_one = norm_one_back(normed_grad)
        input_grads.append((middle_grad + input_ln_grad).astype(jnp.bfloat16))
        current = (
            grad_gain_one,
            grad_shift_one,
            grad_qkv,
            grad_bias_query,
            grad_bias_value,
            grad_out,
            grad_bias_out,
            grad_gain_two,
            grad_shift_two,
            grad_up,
            grad_bias_up,
            grad_down,
            grad_bias_down,
        )
        grad_sums = [
            fresh if before is None else before + fresh for before, fresh in zip(grad_sums, current)
        ]
    reduced = lax.psum_scatter(tuple(grad_sums), ("dp", "seq"), scatter_dimension=0, tiled=True)
    return (jnp.stack(outputs_list)[:, None], jnp.stack(input_grads)[:, None]) + tuple(reduced)


def solution(mesh):
    return jax.shard_map(
        body,
        mesh=mesh,
        in_specs=(
            P(None, "dp", "seq", None),
            P(None, "dp", "seq", None),
            P(None, "dp", None, None),
            P(("dp", "seq")),
            P(("dp", "seq")),
            P(("dp", "seq"), None),
            P(("dp", "seq")),
            P(("dp", "seq")),
            P(("dp", "seq"), None),
            P(("dp", "seq")),
            P(("dp", "seq")),
            P(("dp", "seq")),
            P(("dp", "seq"), None),
            P(("dp", "seq")),
            P(("dp", "seq"), None),
            P(("dp", "seq")),
        ),
        out_specs=(
            P(None, "dp", "seq", None),
            P(None, "dp", "seq", None),
            P(("dp", "seq")),
            P(("dp", "seq")),
            P(("dp", "seq"), None),
            P(("dp", "seq")),
            P(("dp", "seq")),
            P(("dp", "seq"), None),
            P(("dp", "seq")),
            P(("dp", "seq")),
            P(("dp", "seq")),
            P(("dp", "seq"), None),
            P(("dp", "seq")),
            P(("dp", "seq"), None),
            P(("dp", "seq")),
        ),
        check_vma=False,
    )
```

profile of v0, /device:TPU:0, one launch (start us, length us, event | category | flops | bytes accessed | tf_op | source)
XLA Modules:
  0.0 1279.7 jit_solution(13797985035123870307)
XLA Ops:
  15.5 42.8 %all-reduce.19 = (bf16[768]{0:T(1024)(128)(2,1)S(1)}, bf16[768]{0:T(1024)(128)(2,1)S(1)}, bf16[768]{0:T(1024)(128)(2,1)S(1)}, bf16[768]{0:T(1024)(128)(2,1)S(1)}...) all-reduce(bf16[768]{0:T(1024)(128)(2,1)S(1)} %dynamic-update-slice, ...), channel_id=1, replica_groups=mesh['dp'=4,'seq'=8] {'dp','seq'}, use_global_device_ids=true, to_apply=%add.1 | all-reduce | flops 9216 | bytes 36864
  61.4 12.4 all-gather.9.cloned.1.call-done
  87.3 34.4 %all-gather.21.cloned.1.call-done = bf16[1024,768]{1,0:T(8,128)(2,1)} async-done(((bf16[128,768]{1,0:T(8,128)(2,1)}), bf16[1024,768]{1,0:T(8,128)(2,1)}) %all-gather.21.cloned.1.call-update) | async-done | bytes 1572880 | tf_op jit(solution)/shard_map/all_gather | solution.py:240
  124.3 42.7 %all-gather.23.cloned.1.call-done = bf16[1024,768]{1,0:T(8,128)(2,1)} async-done(((bf16[128,768]{1,0:T(8,128)(2,1)}), bf16[1024,768]{1,0:T(8,128)(2,1)}) %all-gather.23.cloned.1.call-update) | async-done | bytes 1572880 | tf_op jit(solution)/shard_map/all_gather | solution.py:239
  169.6 15.7 %while.81 = (s32[]{:T(128)}, f32[128,12,64]{0,2,1:T(8,128)}, f32[12,128]{1,0:T(8,128)S(1)}, bf16[1024,768]{0,1:T(8,128)(2,1)}, s32[2,2]{0,1:T(2,128)}, /*index=5...) while((s32[]{:T(128)}, f32[128,12,64]{0,2,1:T(8,128)}, ...), condition=%wide.region_15.16_spmd.clone, body=%wide.region_11.0_spmd.clone.sunk | while | flops 206512768 | bytes 12520018 | solution.py:89
  186.4 35.8 %all-gather.15.cloned.1.call-done = bf16[768,768]{1,0:T(8,128)(2,1)} async-done(((bf16[24,768]{1,0:T(8,128)(2,1)}), bf16[768,768]{1,0:T(8,128)(2,1)}) %all-gather.15.cloned.1.call-update) | async-done | bytes 1179664 | tf_op jit(solution)/shard_map/all_gather | solution.py:194
  225.4 42.5 %all-gather.11.cloned.1.call-done = bf16[1024,768]{1,0:T(8,128)(2,1)} async-done(((bf16[128,768]{1,0:T(8,128)(2,1)}), bf16[1024,768]{1,0:T(8,128)(2,1)}) %all-gather.11.cloned.1.call-update) | async-done | bytes 1572880 | tf_op jit(solution)/shard_map/all_gather | solution.py:240
  270.5 42.0 %all-gather.13.cloned.1.call-done = bf16[1024,768]{1,0:T(8,128)(2,1)} async-done(((bf16[128,768]{1,0:T(8,128)(2,1)}), bf16[1024,768]{1,0:T(8,128)(2,1)}) %all-gather.13.cloned.1.call-update) | async-done | bytes 1572880 | tf_op jit(solution)/shard_map/all_gather | solution.py:239
  315.2 14.2 %while.80 = (s32[]{:T(128)}, f32[128,12,64]{0,2,1:T(8,128)}, f32[12,128]{1,0:T(8,128)S(1)}, bf16[1024,768]{0,1:T(8,128)(2,1)}, s32[2,2]{0,1:T(2,128)}, /*index=5...) while((s32[]{:T(128)}, f32[128,12,64]{0,2,1:T(8,128)}, ...), condition=%wide.region_6.7_spmd.clone, body=%wide.region_2.6_spmd.clone.sunk | while | flops 206512768 | bytes 12233242 | solution.py:89
  332.6 44.8 %all-gather.17.cloned.1.call-done = bf16[768,3072]{1,0:T(8,128)(2,1)} async-done(((bf16[24,3072]{1,0:T(8,128)(2,1)}), bf16[768,3072]{1,0:T(8,128)(2,1)}) %all-gather.17.cloned.1.call-update) | async-done | bytes 4718608 | tf_op jit(solution)/shard_map/all_gather | solution.py:198
  377.5 8.7 multiply_convert_fusion
  386.2 6.4 multiply_convert_fusion.1
  392.6 49.6 %all-gather.19.cloned.1.call-done = bf16[3072,768]{1,0:T(8,128)(2,1)} async-done(((bf16[96,768]{1,0:T(8,128)(2,1)}), bf16[3072,768]{1,0:T(8,128)(2,1)}) %all-gather.19.cloned.1.call-update) | async-done | bytes 4718608 | tf_op jit(solution)/shard_map/all_gather | solution.py:200
  461.9 28.4 %while.83 = (s32[]{:T(128)}, f32[128,12,64]{0,2,1:T(8,128)}, bf16[1024,768]{0,1:T(8,128)(2,1)}, bf16[1024,768]{0,1:T(8,128)(2,1)}, bf16[1024,768]{0,1:T(8,128)(2...) while((s32[]{:T(128)}, f32[128,12,64]{0,2,1:T(8,128)}, ...), condition=%wide.region_35.36_spmd.clone, body=%wide.region_32.35_spmd.clone.sunk | while | flops 510958720 | bytes 62874448 | solution.py:141
  499.8 28.5 %while.82 = (s32[]{:T(128)}, f32[128,12,64]{0,2,1:T(8,128)}, bf16[1024,768]{0,1:T(8,128)(2,1)}, bf16[1024,768]{0,1:T(8,128)(2,1)}, bf16[1024,768]{0,1:T(8,128)(2...) while((s32[]{:T(128)}, f32[128,12,64]{0,2,1:T(8,128)}, ...), condition=%wide.region_24.25_spmd.clone, body=%wide.region_21.24_spmd.clone.sunk | while | flops 510958720 | bytes 61301528 | solution.py:141
  539.3 17.9 %reduce-scatter.31.cloned.1.call-done = bf16[128,768]{1,0:T(8,128)(2,1)} async-done(((bf16[1024,768]{1,0:T(8,128)(2,1)}), bf16[128,768]{1,0:T(8,128)(2,1)}) %reduce-scatter.31.cloned.1.call-update) | async-done | bytes 196624
  558.3 66.6 %reduce-scatter.29.cloned.1.call-done = bf16[128,768]{1,0:T(8,128)(2,1)} async-done(((bf16[1024,768]{1,0:T(8,128)(2,1)}), bf16[128,768]{1,0:T(8,128)(2,1)}) %reduce-scatter.29.cloned.1.call-update) | async-done | bytes 196624
  625.9 66.7 %reduce-scatter.27.cloned.1.call-done = bf16[128,768]{1,0:T(8,128)(2,1)} async-done(((bf16[1024,768]{1,0:T(8,128)(2,1)}), bf16[128,768]{1,0:T(8,128)(2,1)}) %reduce-scatter.27.cloned.1.call-update) | async-done | bytes 196624
  693.7 66.6 %reduce-scatter.25.cloned.1.call-done = bf16[128,768]{1,0:T(8,128)(2,1)} async-done(((bf16[1024,768]{1,0:T(8,128)(2,1)}), bf16[128,768]{1,0:T(8,128)(2,1)}) %reduce-scatter.25.cloned.1.call-update) | async-done | bytes 196624
  803.8 40.7 %all-reduce.18 = (f32[768]{0:T(1024)S(1)}, f32[768]{0:T(1024)S(1)}, f32[768]{0:T(1024)S(1)}, f32[768]{0:T(1024)S(1)}, f32[768]{0:T(1024)S(1)}, /*index=5*/f32[76...) all-reduce(f32[768]{0:T(1024)S(1)} %add.789, ...), channel_id=6, replica_groups=mesh['dp'=4,'seq'=8] {'dp','seq'}, use_global_device_ids=true, to_apply=%region_42.43.clone | all-reduce | flops 9216 | bytes 73728
  850.9 14.1 %reduce-scatter.19.cloned.1.call-done = f32[24,768]{1,0:T(8,128)} async-done(((f32[768,768]{1,0:T(8,128)}), f32[24,768]{1,0:T(8,128)}) %reduce-scatter.19.cloned.1.call-update) | async-done | bytes 73744 | tf_op jit(solution)/shard_map/reduce_scatter | solution.py:339
  865.0 124.8 %reduce-scatter.17.cloned.1.call-done = f32[24,2304]{1,0:T(8,128)} async-done(((f32[768,2304]{1,0:T(8,128)}), f32[24,2304]{1,0:T(8,128)}) %reduce-scatter.17.cloned.1.call-update) | async-done | bytes 221200 | tf_op jit(solution)/shard_map/reduce_scatter | solution.py:339
  989.7 141.4 %reduce-scatter.21.cloned.1.call-done = f32[24,3072]{1,0:T(8,128)} async-done(((f32[768,3072]{1,0:T(8,128)}), f32[24,3072]{1,0:T(8,128)}) %reduce-scatter.21.cloned.1.call-update) | async-done | bytes 294928 | tf_op jit(solution)/shard_map/reduce_scatter | solution.py:339
  1131.2 141.5 %reduce-scatter.23.cloned.1.call-done = f32[96,768]{1,0:T(8,128)} async-done(((f32[3072,768]{1,0:T(8,128)}), f32[96,768]{1,0:T(8,128)}) %reduce-scatter.23.cloned.1.call-update) | async-done | bytes 294928 | tf_op jit(solution)/shard_map/reduce_scatter | solution.py:339
  (575 shorter events, 220.8 us)
Async XLA Ops:
  7.2 66.6 %all-gather.9.cloned.1.call-start = ((), (), s32[]{:S(2)}) async-start(), calls=%async_computation.8 | async-start | bytes 3649536 | tf_op jit(solution)/shard_map/all_gather | solution.py:191
  7.9 113.7 %all-gather.21.cloned.1.call-start = ((), (), s32[]{:S(2)}) async-start(), calls=%async_computation.14 | async-start | bytes 1769472 | tf_op jit(solution)/shard_map/all_gather | solution.py:240
  78.5 88.5 %all-gather.23.cloned.1.call-start = ((), (), s32[]{:S(2)}) async-start(), calls=%async_computation.15 | async-start | bytes 1769472 | tf_op jit(solution)/shard_map/all_gather | solution.py:239
  79.3 142.9 %all-gather.15.cloned.1.call-start = ((), (), s32[]{:S(2)}) async-start(), calls=%async_computation.11 | async-start | bytes 1216512 | tf_op jit(solution)/shard_map/all_gather | solution.py:194
  79.9 188.1 %all-gather.11.cloned.1.call-start = ((), (), s32[]{:S(2)}) async-start(), calls=%async_computation.9 | async-start | bytes 1769472 | tf_op jit(solution)/shard_map/all_gather | solution.py:240
  80.4 232.1 %all-gather.13.cloned.1.call-start = ((), (), s32[]{:S(2)}) async-start(), calls=%async_computation.10 | async-start | bytes 1769472 | tf_op jit(solution)/shard_map/all_gather | solution.py:239
  81.2 296.2 %all-gather.17.cloned.1.call-start = ((), (), s32[]{:S(2)}) async-start(), calls=%async_computation.12 | async-start | bytes 4866048 | tf_op jit(solution)/shard_map/all_gather | solution.py:198
  82.0 360.3 %all-gather.19.cloned.1.call-start = ((), (), s32[]{:S(2)}) async-start(), calls=%async_computation.13 | async-start | bytes 4866048 | tf_op jit(solution)/shard_map/all_gather | solution.py:200
  82.7 474.5 %reduce-scatter.31.cloned.1.call-start = ((), (), s32[]{:S(2)}) async-start(), calls=%async_computation.23 | async-start | bytes 1769472
  493.0 131.9 %reduce-scatter.29.cloned.1.call-start = ((), (), s32[]{:S(2)}) async-start(), calls=%async_computation.22 | async-start | bytes 1769472
  497.1 195.6 %reduce-scatter.27.cloned.1.call-start = ((), (), s32[]{:S(2)}) async-start(), calls=%async_computation.21 | async-start | bytes 1769472
  530.9 229.4 %reduce-scatter.25.cloned.1.call-start = ((), (), s32[]{:S(2)}) async-start(), calls=%async_computation.20 | async-start | bytes 1769472
  534.0 331.0 %reduce-scatter.19.cloned.1.call-start = ((), (), s32[]{:S(2)}) async-start(), calls=%async_computation.17 | async-start | bytes 2433024 | tf_op jit(solution)/shard_map/reduce_scatter | solution.py:339
  537.3 224.1 %copy-start.8 = (bf16[2,1,128,768]{3,2,1,0:T(8,128)(2,1)S(1)}, bf16[2,1,128,768]{3,2,1,0:T(8,128)(2,1)}, u32[]{:S(2)}) copy-start(bf16[2,1,128,768]{3,2,1,0:T(8,128)(2,1)} %param.24) | copy-start | bytes 1179652
  537.3 224.1 %copy-start.69 = (f32[768]{0:T(1024)S(1)}, f32[768]{0:T(1024)}, u32[]{:S(2)}) copy-start(f32[768]{0:T(1024)} %copy-done.68) | copy-start | bytes 9220
  537.4 224.1 %copy-start.74 = (f32[768]{0:T(1024)S(1)}, f32[768]{0:T(1024)}, u32[]{:S(2)}) copy-start(f32[768]{0:T(1024)} %copy-done.73) | copy-start | bytes 9220
  537.4 224.1 %copy-start.81 = (f32[128]{0:T(128)S(1)}, f32[128]{0:T(128)}, u32[]{:S(2)}) copy-start(f32[128]{0:T(128)} %copy-done.80) | copy-start | bytes 1540
  537.4 224.1 %copy-start.95 = (f32[128]{0:T(128)S(1)}, f32[128]{0:T(128)}, u32[]{:S(2)}) copy-start(f32[128]{0:T(128)} %copy-done.94) | copy-start | bytes 1540
  537.4 452.4 %reduce-scatter.17.cloned.1.call-start = ((), (), s32[]{:S(2)}) async-start(), calls=%async_computation.16 | async-start | bytes 7299072 | tf_op jit(solution)/shard_map/reduce_scatter | solution.py:339
  538.5 224.3 %copy-start.62 = (bf16[128,12,64]{0,2,1:T(8,128)(2,1)}, bf16[128,12,64]{0,2,1:T(8,128)(2,1)S(1)}, u32[]{:S(2)}) copy-start(bf16[128,12,64]{0,2,1:T(8,128)(2,1)S(1)} %get-tuple-element.1526) | copy-start | bytes 589828
  539.3 223.5 %copy-start.66 = (bf16[128,12,64]{0,2,1:T(8,128)(2,1)}, bf16[128,12,64]{0,2,1:T(8,128)(2,1)S(1)}, u32[]{:S(2)}) copy-start(bf16[128,12,64]{0,2,1:T(8,128)(2,1)S(1)} %get-tuple-element.1528) | copy-start | bytes 589828
  625.9 136.9 %copy-start.60 = (bf16[128,768]{0,1:T(8,128)(2,1)}, bf16[128,768]{0,1:T(8,128)(2,1)S(1)}, u32[]{:S(2)}) copy-start(bf16[128,768]{0,1:T(8,128)(2,1)S(1)} %copy.152) | copy-start | bytes 589828
  767.1 364.1 %reduce-scatter.21.cloned.1.call-start = ((), (), s32[]{:S(2)}) async-start(), calls=%async_computation.18 | async-start | bytes 9732096 | tf_op jit(solution)/shard_map/reduce_scatter | solution.py:339
  775.0 497.7 %reduce-scatter.23.cloned.1.call-start = ((), (), s32[]{:S(2)}) async-start(), calls=%async_computation.19 | async-start | bytes 9732096 | tf_op jit(solution)/shard_map/reduce_scatter | solution.py:339
  (132 other events, 1557.9 us)
Sparse Core Ops, SparseCore 0:
  10.9 62.7 all-gather.8
  78.6 42.9 all-gather.20
  124.4 42.5 all-gather.22
  169.7 52.4 all-gather.14
  224.8 43.0 all-gather.10
  269.9 42.5 all-gather.12
  315.4 61.9 all-gather.16
  380.4 61.8 all-gather.18
  493.1 64.0 reduce-scatter.30
  560.5 64.3 reduce-scatter.28
  628.3 64.3 reduce-scatter.26
  695.9 64.3 reduce-scatter.24
  766.2 98.7 reduce-scatter.18
  871.1 118.6 reduce-scatter.16
  996.1 135.0 reduce-scatter.20
  1137.5 135.1 reduce-scatter.22
where the time goes:
time: 1290 us; the launch traced here: 1280 us
  waiting for transfers between devices  947 us (73%)
  matrix products  110 us (9%)
  local copies, waits for them, and re-layouts  94 us (7%)
  blocking collectives  83.5 us (6%)
  other arithmetic  26.8 us (2%)
  between operations  15.8 us (1%)
    reduce_scatter x4, waiting for transfers between devices, body(): lax.psum_scatter(tuple(grad_sums), ('dp', 'seq'), scatter_dimension=0, ti...  422 us
    unnamed x20, waiting for transfers between devices  221 us
    all_gather x2, waiting for transfers between devices, body(): lax.all_gather(keys_now, 'seq', axis=0, tiled=True)  84.7 us
    unnamed x2, blocking collectives  83.5 us
    all_gather x2, waiting for transfers between devices, body(): lax.all_gather(values_now, 'seq', axis=0, tiled=True)  76.9 us
    all_gather x1, waiting for transfers between devices, body(): lax.all_gather(shards[11], ('dp', 'seq'), axis=0, tiled=True)  49.6 us
    unnamed x241, local copies, waits for them, and re-layouts  47 us
    all_gather x1, waiting for transfers between devices, body(): lax.all_gather(shards[9], ('dp', 'seq'), axis=0, tiled=True)  44.8 us
  transfers between devices with their start and end apart: 16, of which 16 were waited for; matrix products, arithmetic and copies ran while one was open for 13% of the time, Pallas kernels for 0%

commit v1 on v0

v1 whole, which is shorter than its diff:
```python
from functools import partial

import jax
import jax.numpy as jnp
from jax import lax
from jax.sharding import PartitionSpec as P

HEADS = 12
HEAD = 64
EPSILON = 1e-05
ALL = ("dp", "seq")


def layer_norm(values, ln_gain, ln_shift):
    center = jnp.mean(values, axis=-1, keepdims=True)
    centered = values - center
    spread = jnp.mean(centered * centered, axis=-1, keepdims=True)
    return centered * lax.rsqrt(spread + EPSILON) * ln_gain + ln_shift


def piece_label(positions, bounds):
    inside = (positions[:, None] >= bounds[None, :, 0]) & (positions[:, None] < bounds[None, :, 1])
    labels = jnp.arange(1, bounds.shape[0] + 1, dtype=jnp.int32)
    return jnp.sum(jnp.where(inside, labels[None, :], 0), axis=1) - 1


def allowed_mask(query_pos, key_pos, bounds):
    query_label = piece_label(query_pos, bounds)
    key_label = piece_label(key_pos, bounds)
    causal = key_pos[None, :] <= query_pos[:, None]
    same_piece = (query_label[:, None] == key_label[None, :]) & (query_label[:, None] >= 0)
    return causal | same_piece


def outer_rows(left, right):
    return lax.dot_general(
        left, right, (((0,), (0,)), ((), ())), preferred_element_type=jnp.float32
    )


def times_transposed(left, right):
    return lax.dot_general(
        left, right, (((1,), (1,)), ((), ())), preferred_element_type=jnp.float32
    )


def pack_layout(width, ff):
    ratio = ff // width
    cols = [3 * width, width, ff, ff]
    offsets = [0]
    for c in cols:
        offsets.append(offsets[-1] + c)
    vec_at = offsets[-1]
    used = vec_at + 8 + ratio
    total = -(-used // 128) * 128
    return offsets, vec_at, ratio, total


def pack_params(params, width, ff):
    ln1_g, ln1_b, w_qkv, b_q, b_v, w_out, b_out, ln2_g, ln2_b, w_up, b_up, w_down, b_down = params
    offsets, vec_at, ratio, total = pack_layout(width, ff)
    rows = w_qkv.shape[0]
    vecs = [ln1_g, ln1_b, b_q, b_v, b_out, ln2_g, ln2_b, b_down]
    pieces = [w_qkv, w_out, w_up, w_down.reshape(rows, ratio * width)]
    pieces += [v.reshape(rows, 1) for v in vecs]
    pieces.append(b_up.reshape(rows, ratio))
    pad = total - (vec_at + 8 + ratio)
    if pad:
        pieces.append(jnp.zeros((rows, pad), pieces[0].dtype))
    return jnp.concatenate(pieces, axis=1)


def unpack_params(packed, width, ff):
    offsets, vec_at, ratio, total = pack_layout(width, ff)
    rows = packed.shape[0]
    w_qkv = packed[:, offsets[0] : offsets[1]]
    w_out = packed[:, offsets[1] : offsets[2]]
    w_up = packed[:, offsets[2] : offsets[3]]
    w_down = packed[:, offsets[3] : offsets[4]].reshape(rows * ratio, width)
    vecs = [packed[:, vec_at + k] for k in range(8)]
    b_up = packed[:, vec_at + 8 : vec_at + 8 + ratio].reshape(rows * ratio)
    ln1_g, ln1_b, b_q, b_v, b_out, ln2_g, ln2_b, b_down = vecs
    return (ln1_g, ln1_b, w_qkv, b_q, b_v, w_out, b_out, ln2_g, ln2_b, w_up, b_up, w_down, b_down)


def unit_bounds(bounds, unit_count, per_device):
    first = lax.axis_index("seq") * per_device
    micro = (first + jnp.arange(per_device, dtype=jnp.int32)) // HEADS
    return bounds[:, 0][micro]


def unit_masks(ubounds, length):
    pos = jnp.arange(length, dtype=jnp.int32)
    return jax.vmap(lambda b: allowed_mask(pos, pos, b))(ubounds)


def rows_to_units(x, seq_count, per_device, parts):
    micro, rows = x.shape[0], x.shape[1]
    x = jnp.transpose(x, (0, 3, 1, 2, 4)).reshape(seq_count, per_device, rows, parts, HEAD)
    x = lax.all_to_all(x, "seq", 0, 0, tiled=True)
    x = jnp.transpose(x, (1, 0, 2, 3, 4))
    return x.reshape(per_device, seq_count * rows, parts, HEAD)


def units_to_rows(x, seq_count, micro, parts):
    per_device, length = x.shape[0], x.shape[1]
    rows = length // seq_count
    x = x.reshape(per_device, seq_count, rows, parts, HEAD)
    x = jnp.transpose(x, (1, 0, 2, 3, 4))
    x = lax.all_to_all(x, "seq", 0, 0, tiled=True)
    x = x.reshape(micro, HEADS, rows, parts, HEAD)
    x = jnp.transpose(x, (0, 2, 3, 1, 4))
    return x.reshape(micro * rows, parts * HEADS * HEAD)


def unit_forward(q, k, v, allowed):
    factor = q.shape[-1] ** (-0.5)
    scores = jnp.einsum("uqd,ukd->uqk", q, k, preferred_element_type=jnp.float32) * factor
    weights = jnp.where(allowed, jnp.exp(scores), 0.0)
    totals = jnp.sum(weights, axis=-1)
    summed = jnp.einsum(
        "uqk,ukd->uqd", weights.astype(jnp.bfloat16), v, preferred_element_type=jnp.float32
    )
    return weights, totals, summed / totals[:, :, None]


def unit_backward(q, k, v, weights, totals, attended, attended_grad):
    factor = q.shape[-1] ** (-0.5)
    grad_f = attended_grad.astype(jnp.float32)
    delta = jnp.sum(grad_f * attended, axis=-1) / totals
    summed_grad = (grad_f / totals[:, :, None]).astype(jnp.bfloat16)
    products = jnp.einsum("uqd,ukd->uqk", summed_grad, v, preferred_element_type=jnp.float32)
    score_grad = (weights * (products - delta[:, :, None])).astype(jnp.bfloat16)
    q_grad = jnp.einsum("uqk,ukd->uqd", score_grad, k, preferred_element_type=jnp.float32) * factor
    k_grad = jnp.einsum("uqk,uqd->ukd", score_grad, q, preferred_element_type=jnp.float32) * factor
    v_grad = jnp.einsum(
        "uqk,uqd->ukd", weights.astype(jnp.bfloat16), summed_grad, preferred_element_type=jnp.float32
    )
    return jnp.stack([q_grad, k_grad, v_grad], axis=2).astype(jnp.bfloat16)


def fallback_attention(queries, keys, values, bounds, row_count):
    micro = bounds.shape[0]
    seq_count = lax.axis_size("seq")
    total_len = row_count * seq_count
    query_pos = lax.axis_index("seq") * row_count + jnp.arange(row_count, dtype=jnp.int32)
    key_pos = jnp.arange(total_len, dtype=jnp.int32)
    saved = []
    attended_all = []
    for m in range(micro):
        sl = slice(m * row_count, (m + 1) * row_count)
        qh = queries[sl].reshape(row_count, HEADS, HEAD)
        k_all = lax.all_gather(keys[sl], "seq", axis=0, tiled=True).reshape(total_len, HEADS, HEAD)
        v_all = lax.all_gather(values[sl], "seq", axis=0, tiled=True).reshape(total_len, HEADS, HEAD)
        allowed = allowed_mask(query_pos, key_pos, bounds[m, 0])
        scores = jnp.einsum("rhd,khd->hrk", qh, k_all, preferred_element_type=jnp.float32) * HEAD ** (-0.5)
        weights = jnp.where(allowed[None], jnp.exp(scores), 0.0)
        totals = jnp.sum(weights, axis=-1)
        summed = jnp.einsum(
            "hrk,khd->rhd", weights.astype(jnp.bfloat16), v_all, preferred_element_type=jnp.float32
        )
        attended = summed / totals.T[:, :, None]
        saved.append((qh, k_all, v_all, weights, totals, attended))
        attended_all.append(attended.reshape(row_count, HEADS * HEAD))
    return jnp.concatenate(attended_all, axis=0), saved


def fallback_attention_backward(saved, attended_grad, row_count):
    factor = HEAD ** (-0.5)
    proj = []
    for m, (qh, k_all, v_all, weights, totals, attended) in enumerate(saved):
        grad = attended_grad[m * row_count : (m + 1) * row_count].astype(jnp.float32)
        grad = grad.reshape(row_count, HEADS, HEAD)
        delta = jnp.sum(grad * attended, axis=-1).T / totals
        grad_heads = (grad / totals.T[:, :, None]).astype(jnp.bfloat16)
        products = jnp.einsum("rhd,khd->hrk", grad_heads, v_all, preferred_element_type=jnp.float32)
        score_grad = (weights * (products - delta[:, :, None])).astype(jnp.bfloat16)
        q_grad = jnp.einsum("hrk,khd->rhd", score_grad, k_all, preferred_element_type=jnp.float32) * factor
        k_rows = jnp.einsum("hrk,rhd->khd", score_grad, qh, preferred_element_type=jnp.float32) * factor
        v_rows = jnp.einsum(
            "hrk,rhd->khd", weights.astype(jnp.bfloat16), grad_heads, preferred_element_type=jnp.float32
        )
        width = HEADS * HEAD
        k_own = lax.psum_scatter(
            k_rows.reshape(-1, width).astype(jnp.bfloat16), "seq", scatter_dimension=0, tiled=True
        )
        v_own = lax.psum_scatter(
            v_rows.reshape(-1, width).astype(jnp.bfloat16), "seq", scatter_dimension=0, tiled=True
        )
        proj.append(
            jnp.concatenate(
                [q_grad.reshape(row_count, width).astype(jnp.bfloat16), k_own, v_own], axis=1
            )
        )
    return jnp.concatenate(proj, axis=0)


def body(inputs, cotangent, bounds, *shards):
    micro = inputs.shape[0]
    row_count = inputs.shape[2]
    width = inputs.shape[3]
    ff = shards[9].shape[1]
    rows = micro * row_count
    seq_count = lax.axis_size("seq")
    unit_count = micro * HEADS
    head_parallel = unit_count % seq_count == 0
    per_device = unit_count // seq_count

    packed = lax.all_gather(pack_params(shards, width, ff), ALL, axis=0, tiled=True)
    (
        gain_one,
        shift_one,
        proj_qkv,
        bias_query,
        bias_value,
        proj_out,
        bias_out,
        gain_two,
        shift_two,
        proj_up,
        bias_up,
        proj_down,
        bias_down,
    ) = unpack_params(packed, width, ff)

    seq_in = inputs[:, 0].reshape(rows, width).astype(jnp.float32)
    normed_f, norm_one_back = jax.vjp(
        layer_norm, seq_in, gain_one.astype(jnp.float32), shift_one.astype(jnp.float32)
    )
    normed = normed_f.astype(jnp.bfloat16)
    projected = jnp.dot(normed, proj_qkv, preferred_element_type=jnp.float32)
    queries = (projected[:, :width] + bias_query.astype(jnp.float32)).astype(jnp.bfloat16)
    keys_now = projected[:, width : 2 * width].astype(jnp.bfloat16)
    values_now = (projected[:, 2 * width :] + bias_value.astype(jnp.float32)).astype(jnp.bfloat16)

    if head_parallel:
        qkv_rows = jnp.concatenate([queries, keys_now, values_now], axis=1)
        qkv_units = rows_to_units(
            qkv_rows.reshape(micro, row_count, 3, HEADS, HEAD), seq_count, per_device, 3
        )
        uq, uk, uv = qkv_units[:, :, 0], qkv_units[:, :, 1], qkv_units[:, :, 2]
        allowed = unit_masks(unit_bounds(bounds, unit_count, per_device), seq_count * row_count)
        weights, totals, attended_u = unit_forward(uq, uk, uv, allowed)
        attended_b = units_to_rows(
            attended_u.astype(jnp.bfloat16)[:, :, None], seq_count, micro, 1
        )
    else:
        attended, saved = fallback_attention(queries, keys_now, values_now, bounds, row_count)
        attended_b = attended.astype(jnp.bfloat16)

    branch = jnp.dot(attended_b, proj_out, preferred_element_type=jnp.float32) + bias_out.astype(
        jnp.float32
    )
    middle = seq_in + branch
    normed_two_f, norm_two_back = jax.vjp(
        layer_norm, middle, gain_two.astype(jnp.float32), shift_two.astype(jnp.float32)
    )
    normed_two = normed_two_f.astype(jnp.bfloat16)
    hidden = jnp.dot(normed_two, proj_up, preferred_element_type=jnp.float32) + bias_up.astype(
        jnp.float32
    )
    activated_f, gelu_back = jax.vjp(partial(jax.nn.gelu, approximate=False), hidden)
    activated = activated_f.astype(jnp.bfloat16)
    mlp_out = jnp.dot(activated, proj_down, preferred_element_type=jnp.float32) + bias_down.astype(
        jnp.float32
    )
    outputs = (middle + mlp_out).astype(jnp.bfloat16)

    out_grad = cotangent[:, 0].reshape(rows, width)
    out_grad_f = out_grad.astype(jnp.float32)
    grad_down = outer_rows(activated, out_grad)
    grad_bias_down = jnp.sum(out_grad_f, axis=0)
    act_grad = times_transposed(out_grad, proj_down)
    (hidden_grad,) = gelu_back(act_grad)
    hidden_grad_b = hidden_grad.astype(jnp.bfloat16)
    grad_up = outer_rows(normed_two, hidden_grad_b)
    grad_bias_up = jnp.sum(hidden_grad_b.astype(jnp.float32), axis=0)
    normed_two_grad = times_transposed(hidden_grad_b, proj_up)
    middle_ln_grad, grad_gain_two, grad_shift_two = norm_two_back(normed_two_grad)
    middle_grad = out_grad_f + middle_ln_grad
    branch_grad = middle_grad.astype(jnp.bfloat16)
    grad_out = outer_rows(attended_b, branch_grad)
    grad_bias_out = jnp.sum(branch_grad.astype(jnp.float32), axis=0)
    attended_grad = times_transposed(branch_grad, proj_out).astype(jnp.bfloat16)

    if head_parallel:
        grad_units = rows_to_units(
            attended_grad.reshape(micro, row_count, 1, HEADS, HEAD), seq_count, per_device, 1
        )[:, :, 0]
        qkv_grad_u = unit_backward(uq, uk, uv, weights, totals, attended_u, grad_units)
        proj_grad = units_to_rows(qkv_grad_u, seq_count, micro, 3)
    else:
        proj_grad = fallback_attention_backward(saved, attended_grad, row_count)

    grad_qkv = outer_rows(normed, proj_grad)
    grad_bias_query = jnp.sum(proj_grad[:, :width].astype(jnp.float32), axis=0)
    grad_bias_value = jnp.sum(proj_grad[:, 2 * width :].astype(jnp.float32), axis=0)
    normed_grad = times_transposed(proj_grad, proj_qkv)
    input_ln_grad, grad_gain_one, grad_shift_one = norm_one_back(normed_grad)
    input_grads = (middle_grad + input_ln_grad).astype(jnp.bfloat16)

    grads = (
        grad_gain_one,
        grad_shift_one,
        grad_qkv,
        grad_bias_query,
        grad_bias_value,
        grad_out,
        grad_bias_out,
        grad_gain_two,
        grad_shift_two,
        grad_up,
        grad_bias_up,
        grad_down,
        grad_bias_down,
    )
    packed_grads = pack_params(tuple(g.astype(jnp.bfloat16) for g in grads), width, ff)
    reduced = lax.psum_scatter(packed_grads, ALL, scatter_dimension=0, tiled=True)
    reduced = tuple(g.astype(jnp.float32) for g in unpack_params(reduced, width, ff))
    return (
        outputs.reshape(micro, 1, row_count, width),
        input_grads.reshape(micro, 1, row_count, width),
    ) + reduced


def solution(mesh):
    vec = P(ALL)
    mat = P(ALL, None)
    param_specs = (vec, vec, mat, vec, vec, mat, vec, vec, vec, mat, vec, mat, vec)
    return jax.shard_map(
        body,
        mesh=mesh,
        in_specs=(P(None, "dp", "seq", None), P(None, "dp", "seq", None), P(None, "dp", None, None))
        + param_specs,
        out_specs=(P(None, "dp", "seq", None), P(None, "dp", "seq", None)) + param_specs,
        check_vma=False,
    )
```

time: 1290 us -> 613 us (0.48)
  waiting for transfers between devices: 947 us -> 375 us
  blocking collectives: 83.5 us -> 17.7 us
  matrix products: 110 us -> 74.1 us
    reduce_scatter x4 -> x0, waiting for transfers between devices: 422 us -> none  [body(): lax.psum_scatter(tuple(grad_sums), ('dp', 'seq'), scatter_dimension=0, ti...]
    all_gather x8 -> x1, waiting for transfers between devices: 304 us -> 104 us  [body(): lax.all_gather(pack_params(shards, width, ff), ALL, axis=0, tiled=True)]
    unnamed x2 -> x0, blocking collectives: 83.5 us -> none
    unnamed x241 -> x73, local copies, waits for them, and re-layouts: 47 us -> 4.07 us
    reshape x2 -> x20, local copies, waits for them, and re-layouts: 0.31 us -> 31.5 us  [the longest x12 10.1 us: pack_params(): pieces += [v.reshape(rows, 1) for v in vecs]]
    all_to_all x0 -> x3, waiting for transfers between devices: none -> 26.5 us  [the longest x1 26.4 us: rows_to_units(): x = lax.all_to_all(x, 'seq', 0, 0, tiled=True)]
    concatenate x0 -> x3, local copies, waits for them, and re-layouts: none -> 26.1 us  [the longest x2 25.5 us: pack_params(): return jnp.concatenate(pieces, axis=1)]
    unnamed x20 -> x3, waiting for transfers between devices: 221 us -> 245 us
  transfers between devices with their start and end apart: 16 -> 5, of which waited for: 16 -> 3; matrix products, arithmetic and copies ran while one was open for 13% -> 9% of each run, Pallas kernels for 0% -> 0%
where the time goes in v1:
time: 613 us; the launch traced here: 603 us
  waiting for transfers between devices  375 us (61%)
  local copies, waits for them, and re-layouts  85.6 us (14%)
  matrix products  74.1 us (12%)
  other arithmetic  22.6 us (4%)
  blocking collectives  17.7 us (3%)
  between operations  15.2 us (2%)
  starting transfers between devices  12.2 us (2%)
    unnamed x3, waiting for transfers between devices  245 us
    all_gather x1, waiting for transfers between devices, body(): lax.all_gather(pack_params(shards, width, ff), ALL, axis=0, tiled=True)  104 us
    all_to_all x1, waiting for transfers between devices, rows_to_units(): x = lax.all_to_all(x, 'seq', 0, 0, tiled=True)  26.4 us
    concatenate x2, local copies, waits for them, and re-layouts, pack_params(): return jnp.concatenate(pieces, axis=1)  25.5 us
    all_to_all x1, blocking collectives, rows_to_units(): x = lax.all_to_all(x, 'seq', 0, 0, tiled=True)  17.7 us
    dot_general x4, matrix products, outer_rows(): lax.dot_general(left, right, (((0,), (0,)), ((), ())), preferred_element_...  14.7 us
    dot_general x4, matrix products, times_transposed(): lax.dot_general(left, right, (((1,), (1,)), ((), ())), preferred_element_...  12.9 us
  transfers between devices with their start and end apart: 5, of which 3 were waited for; matrix products, arithmetic and copies ran while one was open for 9% of the time, Pallas kernels for 0%

profile of v1, /device:TPU:0, one launch (start us, length us, event | category | flops | bytes accessed | tf_op | source)
XLA Modules:
  0.0 602.6 jit_solution(15129525905358120235)
XLA Ops:
  19.4 103.8 %all-gather.2.cloned.1.call-done = bf16[768,9344]{1,0:T(8,128)(2,1)} async-done(((bf16[24,9344]{1,0:T(8,128)(2,1)}), bf16[768,9344]{1,0:T(8,128)(2,1)}) %all-gather.2.cloned.1.call-update) | async-done | bytes 14352400 | tf_op jit(solution)/shard_map/all_gather | solution.py:209
  123.2 3.4 convert_reduce_fusion.1
  126.9 3.1 fusion.19
  132.5 3.9 all-to-all-start
  139.0 26.4 %all-to-all-done = bf16[8,3,128,3,64]{2,4,3,1,0:T(8,128)(2,1)S(1)} async-done(((bf16[8,3,128,3,64]{2,4,3,1,0:T(8,128)(2,1)}), bf16[8,3,128,3,64]{2,4,3,1,0:T(8,128)(2,1)S(1)}, u32[]{:S(2)}, u32[]{:S(2)}) %all-to-all-start) | async-done | bytes 1179680 | tf_op jit(solution)/shard_map/all_to_all | solution.py:100
  166.8 6.6 %fusion.53 = (f32[3,1024]{1,0:T(4,128)S(1)}, f32[3,1024,1024]{1,2,0:T(8,128)S(1)}) fusion(bf16[3,1024,3,64]{1,3,0,2:T(8,128)(2,1)S(1)} %reshape.442, pred[3,1024]{1,0:T(4,128)(4,1)S(1)} %broadcast_compare_fusion, s32[3,1024]{1,0:T(4,128)S(1)} %broadcast_add_fusion, pred[1024,1024]{0,1:T(8,128)(4,1)} %iota_compare_fusion), kind=kOutput, calls=%fused_computation.139 | convolution fusion | flops 421524480 | bytes 14467072 | tf_op jit(solution)/shard_map/uqd,ukd->uqk/dot_general | solution.py:118
  179.1 3.8 all-to-all-start.1
  184.2 4.9 slice.168
  189.1 8.5 %reshape.445 = bf16[3072,768]{1,0:T(8,128)(2,1)} reshape(bf16[768,3072]{1,0:T(8,128)(2,1)} %slice.168) | data formatting | bytes 9437184 | tf_op jit(solution)/shard_map/reshape | solution.py:79
  200.3 10.7 %multiply_convert_fusion.1 = (bf16[256,3072]{1,0:T(8,128)(2,1)}, f32[256,3072]{1,0:T(8,128)S(1)}, f32[256,3072]{1,0:T(8,128)S(1)}) fusion(f32[3072]{0:T(1024)S(1)} %reshape.466, bf16[768,9344]{1,0:T(8,128)(2,1)} %all-gather.2.cloned.1.call-done, f32[256,768]{1,0:T(8,128)S(1)} %get-tuple-element.119, f32[768]{0:T(1024)S(1)} %get-tuple-element.84, ...), kind=kOutput, calls=%fused_computation.16 | convolution fusion | flops 1260847104 | bytes 13389824 | tf_op jit(solution)/shard_map/dot_general | solution.py:259
  211.1 2.7 fusion.56
  213.8 5.1 multiply_reduce_fusion
  223.0 17.7 %all_to_all.20 = bf16[8,3,128,1,64]{2,4,3,1,0:T(8,128)(2,1)S(1)} all-to-all(bf16[8,3,128,1,64]{2,4,3,1,0:T(8,128)(2,1)S(1)} %bitcast.179), channel_id=1, replica_groups=mesh['dp'=4,'seq'=8] {'seq'}, dimensions={0} | all-to-all | bytes 786432 | tf_op jit(solution)/shard_map/all_to_all | solution.py:100
  243.5 6.8 %fusion.29 = bf16[3,1024,64]{1,2,0:T(8,128)(2,1)S(1)} fusion(f32[3,1024,1024]{1,2,0:T(8,128)} %copy-done.2, f32[3,1024,64]{1,2,0:T(8,128)S(1)} %reshape.468, f32[3,1024]{1,0:T(4,128)S(1)} %get-tuple-element.114), kind=kOutput, calls=%fused_computation.49 | convolution fusion | flops 406388736 | bytes 13774848 | tf_op jit(solution)/shard_map/uqk,uqd->ukd/dot_general | solution.py:136
  250.5 6.5 %multiply_convert_fusion = bf16[3,1024,1024]{1,2,0:T(8,128)(2,1)S(1)} fusion(f32[3,1024,1024]{1,2,0:T(8,128)} %copy-done.2, f32[3,1024]{1,0:T(4,128)S(1)} %div.84, bf16[3,1024,3,64]{1,3,0,2:T(8,128)(2,1)S(1)} %copy-done.5, f32[3,1024,64]{1,2,0:T(8,128)S(1)} %reshape.468, f32[3,1024]{1,0:T(4,128)S(1)} %get-tuple-element.114), kind=kOutput, calls=%fused_computation.1 | convolution fusion | flops 412483584 | bytes 20086784 | tf_op jit(solution)/shard_map/uqd,ukd->uqk/dot_general | solution.py:132
  261.9 4.4 all-to-all-start.3
  278.7 5.0 convolution_convert_fusion
  283.7 8.5 %reshape.452 = bf16[768,3072]{1,0:T(8,128)(2,1)} reshape(bf16[3072,768]{1,0:T(8,128)(2,1)} %convolution_convert_fusion) | data formatting | bytes 9437184 | tf_op jit(solution)/shard_map/reshape | solution.py:64
  292.2 5.2 convolution_convert_fusion.1
  300.1 3.3 fusion.47
  308.1 3.0 convolution_convert_fusion.2
  311.1 23.6 %concatenate.13 = bf16[768,9344]{1,0:T(8,128)(2,1)} concatenate(bf16[768,2304]{1,0:T(8,128)(2,1)} %convolution_convert_fusion.2, bf16[768,768]{1,0:T(8,128)(2,1)} %copy.160, bf16[768,3072]{1,0:T(8,128)(2,1)} %convolution_convert_fusion.1, bf16[768,3072]{1,0:T(8,128)(2,1)} %reshape.452, bf16[768,1]{1,0:T(8,128)(2,1)} %convert_element_type.404, ...), dimensions={1} | concatenate | bytes 28704768 | tf_op jit(solution)/shard_map/concatenate | solution.py:70
  335.4 5.0 fusion.26
  341.6 244.8 %all-reduce.3.cloned.1.call-done = bf16[768,9344]{1,0:T(8,128)(2,1)} async-done(((bf16[768,9344]{1,0:T(8,128)(2,1)}), bf16[768,9344]{1,0:T(8,128)(2,1)}) %all-reduce.3.cloned.1.call-update) | async-done | bytes 14352400
  (174 shorter events, 70.7 us)
Async XLA Ops:
  7.2 129.3 %copy-start = (s32[2,1,2,2]{3,2,1,0:T(2,128)S(1)}, s32[2,1,2,2]{3,2,1,0:T(2,128)}, u32[]{:S(2)}) copy-start(s32[2,1,2,2]{3,2,1,0:T(2,128)} %param.18) | copy-start | bytes 100
  7.2 119.4 %copy-start.3 = (bf16[2,1,128,768]{3,2,1,0:T(8,128)(2,1)S(1)}, bf16[2,1,128,768]{3,2,1,0:T(8,128)(2,1)}, u32[]{:S(2)}) copy-start(bf16[2,1,128,768]{3,2,1,0:T(8,128)(2,1)} %param.16) | copy-start | bytes 1179652
  7.2 115.9 %all-gather.2.cloned.1.call-start = ((), (), s32[]{:S(2)}) async-start(), calls=%async_computation.4 | async-start | bytes 14800896 | tf_op jit(solution)/shard_map/all_gather | solution.py:209
  18.1 111.9 %copy-start.17 = (f32[256]{0:T(256)}, f32[256]{0:T(256)S(1)}, u32[]{:S(2)}) copy-start(f32[256]{0:T(256)S(1)} %get-tuple-element.112) | copy-start | bytes 3076
  19.3 247.9 %copy-start.21 = (f32[2,128]{1,0:T(2,128)}, f32[2,128]{1,0:T(2,128)S(1)}, u32[]{:S(2)}) copy-start(f32[2,128]{1,0:T(2,128)S(1)} %multiply_reduce_fusion.6) | copy-start | bytes 3076
  19.4 110.6 %copy-start.19 = (f32[256]{0:T(256)}, f32[256]{0:T(256)S(1)}, u32[]{:S(2)}) copy-start(f32[256]{0:T(256)S(1)} %bitcast_rsqrt_fusion) | copy-start | bytes 3076
  132.5 32.9 %all-to-all-start = ((bf16[8,3,128,3,64]{2,4,3,1,0:T(8,128)(2,1)}), bf16[8,3,128,3,64]{2,4,3,1,0:T(8,128)(2,1)S(1)}, u32[]{:S(2)}, u32[]{:S(2)}) async-start(bf16[8,3,128,3,64]{2,4,3,1,0:T(8,128)(2,1)} %bitcast.16), calls=%async_computation | async-start | bytes 2359296 | tf_op jit(solution)/shard_map/all_to_all | solution.py:100
  179.1 18.5 %all-to-all-start.1 = ((bf16[8,3,128,1,64]{2,4,3,1,0:T(8,128)(2,1)}), bf16[8,3,128,1,64]{2,4,3,1,0:T(8,128)(2,1)S(1)}, u32[]{:S(2)}, u32[]{:S(2)}) async-start(bf16[8,3,128,1,64]{2,4,3,1,0:T(8,128)(2,1)} %bitcast.159), calls=%async_computation.1 | async-start | bytes 786432 | tf_op jit(solution)/shard_map/all_to_all | solution.py:110
  198.0 13.1 %copy-start.8 = (bf16[2,128,1,12,64]{1,0,4,3,2:T(2,128)(2,1)}, bf16[2,128,1,12,64]{1,0,4,3,2:T(2,128)(2,1)S(1)}, u32[]{:S(2)}) copy-start(bf16[2,128,1,12,64]{1,0,4,3,2:T(2,128)(2,1)S(1)} %copy.148) | copy-start | bytes 1179652
  198.0 13.0 %slice-start = ((s8[4718592]{0:T(1024)(128)(4,1)}), s8[4194304]{0:T(1024)(128)(4,1)S(1)}, s32[]{:S(2)}) async-start(s8[4718592]{0:T(1024)(128)(4,1)} %bitcast.167), calls=%async_computation.6 | async-start | bytes 8388608
  200.1 18.9 %copy-start.15 = (f32[256]{0:T(256)}, f32[256]{0:T(256)S(1)}, u32[]{:S(2)}) copy-start(f32[256]{0:T(256)S(1)} %broadcast_multiply_fusion) | copy-start | bytes 3076
  200.3 18.7 %copy-start.23 = (f32[256]{0:T(256)}, f32[256]{0:T(256)S(1)}, u32[]{:S(2)}) copy-start(f32[256]{0:T(256)S(1)} %fusion.42) | copy-start | bytes 3076
  200.3 10.7 %copy-start.6 = (bf16[2,1,128,768]{3,2,1,0:T(8,128)(2,1)S(1)}, bf16[2,1,128,768]{3,2,1,0:T(8,128)(2,1)}, u32[]{:S(2)}) copy-start(bf16[2,1,128,768]{3,2,1,0:T(8,128)(2,1)} %param.17) | copy-start | bytes 1179652
  200.3 10.7 %slice-start.1 = ((s8[4718592]{0:T(1024)(128)(4,1)}), s8[524288]{0:T(1024)(128)(4,1)S(1)}, s32[]{:S(2)}) async-start(s8[4718592]{0:T(1024)(128)(4,1)} %bitcast.167), calls=%async_computation.7 | async-start | bytes 1048576
  243.5 6.8 %copy-start.7 = (f32[3,1024,64]{1,2,0:T(8,128)S(1)}, f32[3,1024,64]{1,2,0:T(8,128)}, u32[]{:S(2)}) copy-start(f32[3,1024,64]{1,2,0:T(8,128)} %get-tuple-element.117) | copy-start | bytes 2359300
  243.5 7.0 %copy-start.5 = (bf16[3,1024,3,64]{1,3,0,2:T(8,128)(2,1)S(1)}, bf16[3,1024,3,64]{1,3,0,2:T(8,128)(2,1)}, u32[]{:S(2)}) copy-start(bf16[3,1024,3,64]{1,3,0,2:T(8,128)(2,1)} %copy-done.4) | copy-start | bytes 3538948
  260.6 6.7 %copy-start.14 = (f32[768]{0:T(1024)S(1)}, f32[768]{0:T(1024)}, u32[]{:S(2)}) copy-start(f32[768]{0:T(1024)} %copy-done.13) | copy-start | bytes 9220
  261.9 12.6 %copy-start.9 = (bf16[2,128,1,12,64]{1,0,4,3,2:T(2,128)(2,1)S(1)}, bf16[2,128,1,12,64]{1,0,4,3,2:T(2,128)(2,1)}, u32[]{:S(2)}) copy-start(bf16[2,128,1,12,64]{1,0,4,3,2:T(2,128)(2,1)} %copy-done.8) | copy-start | bytes 1179652
  261.9 12.6 %copy-start.11 = (bf16[256,768]{1,0:T(8,128)(2,1)S(1)}, bf16[256,768]{1,0:T(8,128)(2,1)}, u32[]{:S(2)}) copy-start(bf16[256,768]{1,0:T(8,128)(2,1)} %copy-done.10) | copy-start | bytes 1179652
  261.9 35.5 %all-to-all-start.3 = ((bf16[8,3,128,3,64]{2,4,3,1,0:T(8,128)(2,1)}), bf16[8,3,128,3,64]{2,4,3,1,0:T(8,128)(2,1)}, u32[]{:S(2)}, u32[]{:S(2)}) async-start(bf16[8,3,128,3,64]{2,4,3,1,0:T(8,128)(2,1)} %maximum_bitcast_fusion), calls=%async_computation.3 | async-start | bytes 2359296 | tf_op jit(solution)/shard_map/all_to_all | solution.py:110
  266.3 320.1 %all-reduce.3.cloned.1.call-start = ((), (), s32[]{:S(2)}) async-start(), calls=%async_computation.5 | async-start | bytes 28704768
  283.7 8.5 %copy-start.16 = (f32[256]{0:T(256)S(1)}, f32[256]{0:T(256)}, u32[]{:S(2)}) copy-start(f32[256]{0:T(256)} %copy-done.15) | copy-start | bytes 3076
  283.7 8.5 %copy-start.24 = (f32[256]{0:T(256)S(1)}, f32[256]{0:T(256)}, u32[]{:S(2)}) copy-start(f32[256]{0:T(256)} %copy-done.23) | copy-start | bytes 3076
  335.4 259.9 %copy-start.1 = (s32[2,1,2,2]{3,2,1,0:T(2,128)S(1)}, s32[2,1,2,2]{3,2,1,0:T(2,128)}, u32[]{:S(2)}) copy-start(s32[2,1,2,2]{3,2,1,0:T(2,128)} %param.18) | copy-start | bytes 100
  (15 other events, 53.6 us)
Sparse Core Ops, SparseCore 0:
  17.0 106.0 all-gather.1
  334.9 251.4 all-reduce.2
